TPU v7x, 32 devices: a whole 2x2x4 slice. The times are simulated.
32 devices in a mesh: dp: 4 (over x, core), expert: 8 (over z, y).
Axes of the slice: x: 2, y: 2, z: 4, core: 2. Of those that a mesh axis runs over, the one named last changes fastest.
Arguments:
- inputs: bfloat16 [512, 4096], P(('dp', 'expert')), may hold values from -6 to 6
- grad_out: bfloat16 [512, 4096], P(('dp', 'expert')), may hold values from -0.796875 to 0.796875
- labels: int32 [512, 1], P(('dp', 'expert')), may hold values from 0 to 7; in each aligned block of 16 rows (0 to 15, 16 to 31, ...) at most 3 rows name the same one
- w_gate: bfloat16 [4096, 57344], P('dp', 'expert'), may hold values from -0.09375 to 0.09375
- w_up: bfloat16 [4096, 57344], P('dp', 'expert'), may hold values from -0.09375 to 0.09375
- w_down: bfloat16 [57344, 4096], P('expert', 'dp'), may hold values from -0.0625 to 0.0625
Outputs:
- grad_in: bfloat16 [512, 4096], P(('dp', 'expert'))
- grad_gate: bfloat16 [4096, 57344], P('dp', 'expert')
- grad_up: bfloat16 [4096, 57344], P('dp', 'expert')
- grad_down: bfloat16 [57344, 4096], P('expert', 'dp')
Inputs may be any that keep to these rules, and one draw needn't show every extreme that they name: `labels`: among the 16 rows of one device no expert is named by more than 3 rows, a bound that some block reaches.
All inputs are finite; a program needn't handle non-finite values.
Results may differ from a plain program's by a relative error of at most 0.011.
Values may be sent and summed in bfloat16 or wider, within the bound.
No kernel may reach another device: no remote copies, remote signals or barrier semaphores. Data moves between devices by JAX's collectives and lax.ppermute only.
A program may use at most 192 MiB of HBM per device.

v0:
```python
import jax
import jax.numpy as jnp
from jax import lax
from jax.sharding import PartitionSpec as P

EXPERTS = 8


def nonlinear(gate, up, dhid):
    sig = jax.nn.sigmoid(gate)
    act = gate * sig
    hidden = (act * up).astype(jnp.bfloat16)
    d_up = (dhid * act).astype(jnp.bfloat16)
    d_gate = (dhid * up * sig * (1.0 + gate * (1.0 - sig))).astype(jnp.bfloat16)
    return (hidden, d_up, d_gate)


def contract_rows(left, right):
    return lax.dot_general(
        left, right, (((0,), (0,)), ((), ())), preferred_element_type=jnp.float32
    )


def on_device(inputs, grad_out, labels, w_gate, w_up, w_down):
    members = lax.axis_size("expert")
    replicas = lax.axis_size("dp")
    group = members // EXPERTS
    tok_count = inputs.shape[0]
    width = inputs.shape[1]
    capacity = 3 * tok_count // (2 * EXPERTS)
    label_col = labels[:, 0]
    onehot = (label_col[:, None] == jnp.arange(EXPERTS, dtype=jnp.int32)[None, :]).astype(jnp.int32)
    before = jnp.cumsum(onehot, axis=0) - onehot
    rank_in = jnp.sum(before * onehot, axis=1)
    slot_ids = label_col * capacity + rank_in

    def spread(values):
        buffer = jnp.zeros((EXPERTS * capacity, width), jnp.bfloat16).at[slot_ids].set(values)
        return jnp.repeat(buffer.reshape(EXPERTS, 1, capacity, width), group, axis=0)

    recv_in, recv_grad = (
        lax.all_to_all(
            lax.all_to_all(spread(inputs), "dp", split_axis=3, concat_axis=1, tiled=True),
            "expert",
            split_axis=0,
            concat_axis=0,
            tiled=True,
        ),
        lax.all_to_all(
            lax.all_to_all(spread(grad_out), "dp", split_axis=3, concat_axis=1, tiled=True),
            "expert",
            split_axis=0,
            concat_axis=0,
            tiled=True,
        ),
    )
    columns = width // replicas
    rows_in = recv_in.reshape(-1, columns)
    rows_grad = recv_grad.reshape(-1, columns)
    gate_part = jnp.dot(rows_in, w_gate, preferred_element_type=jnp.float32)
    up_part = jnp.dot(rows_in, w_up, preferred_element_type=jnp.float32)
    dhid_part = lax.dot_general(
        rows_grad, w_down, (((1,), (1,)), ((), ())), preferred_element_type=jnp.float32
    )
    gate, up, dhid = lax.psum((gate_part, up_part, dhid_part), "dp")
    hidden, d_up, d_gate = nonlinear(gate, up, dhid)
    d_rows = lax.dot_general(
        d_gate, w_gate, (((1,), (1,)), ((), ())), preferred_element_type=jnp.float32
    )
    d_rows = d_rows + lax.dot_general(
        d_up, w_up, (((1,), (1,)), ((), ())), preferred_element_type=jnp.float32
    )
    back_rows = lax.all_to_all(
        lax.all_to_all(
            d_rows.reshape(members, replicas, capacity, columns).astype(jnp.bfloat16),
            "dp",
            split_axis=1,
            concat_axis=3,
            tiled=True,
        ),
        "expert",
        split_axis=0,
        concat_axis=0,
        tiled=True,
    ).astype(jnp.float32)
    summed = jnp.sum(back_rows.reshape(EXPERTS, group, capacity, width), axis=1)
    grad_in = summed.reshape(EXPERTS * capacity, width)[slot_ids].astype(jnp.bfloat16)
    grad_gate = contract_rows(rows_in, d_gate).astype(jnp.bfloat16)
    grad_up = contract_rows(rows_in, d_up).astype(jnp.bfloat16)
    grad_down = contract_rows(hidden, rows_grad).astype(jnp.bfloat16)
    return (grad_in, grad_gate, grad_up, grad_down)


def solution(mesh):
    return jax.shard_map(
        on_device,
        mesh=mesh,
        in_specs=(
            P(("dp", "expert"), None),
            P(("dp", "expert"), None),
            P(("dp", "expert"), None),
            P("dp", "expert"),
            P("dp", "expert"),
            P("expert", "dp"),
        ),
        out_specs=(
            P(("dp", "expert"), None),
            P("dp", "expert"),
            P("dp", "expert"),
            P("expert", "dp"),
        ),
        check_vma=False,
    )
```

profile of v0, /device:TPU:0, one launch (start us, length us, event | category | flops | bytes accessed | tf_op | source)
XLA Modules:
  0.0 330.5 jit_solution(10850027350697886702)
XLA Ops:
  7.2 0.7 fusion.7
  7.9 0.8 select_reduce_fusion
  8.8 0.7 fusion.8
  9.4 1.2 scatter_custom_fusion.1
  10.7 0.1 reshape_broadcast_in_dim_reshape.7
  10.8 4.6 %copy.38 = bf16[8,1,3,4096]{0,2,1,3:T(4,128)(2,1)} copy(bf16[8,1,3,4096]{3,2,0,1:T(4,128)(2,1)S(1)} %reshape_broadcast_in_dim_reshape.7) | data formatting | bytes 393216 | tf_op jit(solution)/shard_map/reshape;broadcast_in_dim;reshape | solution.py:39
  15.4 5.8 %reshape.60 = bf16[4,2,12288]{2,1,0:T(2,128)(2,1)} reshape(bf16[4096,1,3,8]{3,2,1,0:T(4,128)(2,1)} %bitcast.43) | data formatting | bytes 393216
  21.2 4.2 %all-to-all-start.2 = ((bf16[4,2,12288]{2,1,0:T(2,128)(2,1)}), bf16[4,2,12288]{2,1,0:T(2,128)(2,1)S(1)}, u32[]{:S(2)}, u32[]{:S(2)}) async-start(bf16[4,2,12288]{2,1,0:T(2,128)(2,1)} %reshape.60), calls=%async_computation.2 | async-start | bytes 393216 | tf_op jit(solution)/shard_map/all_to_all | solution.py:43
  25.4 1.2 scatter_custom_fusion
  26.6 0.1 reshape_broadcast_in_dim_reshape.6
  26.8 4.6 %copy.34 = bf16[8,1,3,4096]{0,2,1,3:T(4,128)(2,1)} copy(bf16[8,1,3,4096]{3,2,0,1:T(4,128)(2,1)S(1)} %reshape_broadcast_in_dim_reshape.6) | data formatting | bytes 393216 | tf_op jit(solution)/shard_map/reshape;broadcast_in_dim;reshape | solution.py:39
  31.4 5.8 %reshape.62 = bf16[4,2,12288]{2,1,0:T(2,128)(2,1)} reshape(bf16[4096,1,3,8]{3,2,1,0:T(4,128)(2,1)} %bitcast.44) | data formatting | bytes 393216
  37.2 0.0 all-to-all-done.2
  37.2 3.4 %all-to-all-start = ((bf16[4,2,12288]{2,1,0:T(2,128)(2,1)}), bf16[4,2,12288]{2,1,0:T(2,128)(2,1)S(1)}, u32[]{:S(2)}, u32[]{:S(2)}) async-start(bf16[4,2,12288]{2,1,0:T(2,128)(2,1)} %reshape.62), calls=%async_computation | async-start | bytes 393216 | tf_op jit(solution)/shard_map/all_to_all | solution.py:50
  40.6 4.8 %reshape.61 = bf16[4096,1,3,8]{3,2,1,0:T(4,128)(2,1)} reshape(bf16[4,2,12288]{2,1,0:T(2,128)(2,1)S(1)} %all-to-all-done.2) | data formatting | bytes 393216
  45.4 6.6 %copy.40 = bf16[8,4,3,1024]{3,1,2,0:T(4,128)(2,1)} copy(bf16[8,4,3,1024]{0,2,3,1:T(4,128)(2,1)} %bitcast.45) | data formatting | bytes 393216 | tf_op jit(solution)/shard_map/all_to_all | solution.py:43
  52.0 0.0 all-to-all-done
  52.0 6.5 %all-to-all-start.3 = ((bf16[8,4,3,1024]{3,1,2,0:T(4,128)(2,1)}), bf16[8,4,3,1024]{3,1,2,0:T(4,128)(2,1)S(1)}, u32[]{:S(2)}, u32[]{:S(2)}) async-start(bf16[8,4,3,1024]{3,1,2,0:T(4,128)(2,1)} %copy.40), calls=%async_computation.3 | async-start | bytes 393216 | tf_op jit(solution)/shard_map/all_to_all | solution.py:42
  58.5 4.8 %reshape.63 = bf16[4096,1,3,8]{3,2,1,0:T(4,128)(2,1)} reshape(bf16[4,2,12288]{2,1,0:T(2,128)(2,1)S(1)} %all-to-all-done) | data formatting | bytes 393216
  63.2 6.7 %copy.36 = bf16[8,4,3,1024]{3,1,2,0:T(4,128)(2,1)} copy(bf16[8,4,3,1024]{0,2,3,1:T(4,128)(2,1)} %bitcast.46) | data formatting | bytes 393216 | tf_op jit(solution)/shard_map/all_to_all | solution.py:50
  69.9 6.0 %all-to-all-start.1 = ((bf16[8,4,3,1024]{3,1,2,0:T(4,128)(2,1)}), bf16[8,4,3,1024]{3,1,2,0:T(4,128)(2,1)S(1)}, u32[]{:S(2)}, u32[]{:S(2)}) async-start(bf16[8,4,3,1024]{3,1,2,0:T(4,128)(2,1)} %copy.36), calls=%async_computation.1 | async-start | bytes 393216 | tf_op jit(solution)/shard_map/all_to_all | solution.py:49
  75.9 0.2 all-reduce.3.cloned.1.call-start
  76.1 0.1 copy.41
  76.2 0.2 reshape.26
  76.4 9.2 %fusion.12 = f32[96,7168]{1,0:T(8,128)} fusion(bf16[96,1024]{1,0:T(8,128)(2,1)S(1)} %reshape.26, bf16[1024,7168]{1,0:T(8,128)(2,1)} %param.9), kind=kOutput, calls=%fused_computation.27 | convolution fusion | flops 1409286144 | bytes 17629184 | tf_op jit(solution)/shard_map/dot_general | solution.py:60
  85.6 9.2 %fusion.11 = f32[96,7168]{1,0:T(8,128)} fusion(bf16[96,1024]{1,0:T(8,128)(2,1)S(1)} %reshape.26, bf16[1024,7168]{1,0:T(8,128)(2,1)} %param.10), kind=kOutput, calls=%fused_computation.26 | convolution fusion | flops 1409286144 | bytes 17629184 | tf_op jit(solution)/shard_map/dot_general | solution.py:61
  94.7 0.0 all-to-all-done.1
  94.7 0.1 copy.37
  94.9 0.2 reshape.25
  95.0 11.3 %fusion.10 = f32[96,7168]{1,0:T(8,128)} fusion(bf16[96,1024]{1,0:T(8,128)(2,1)S(1)} %reshape.25, bf16[7168,1024]{1,0:T(8,128)(2,1)} %param.11), kind=kOutput, calls=%fused_computation.25 | convolution fusion | flops 1409286144 | bytes 17629184 | tf_op jit(solution)/shard_map/dot_general | solution.py:62
  106.3 0.0 all-reduce.3.cloned.1.call-update
  106.4 153.3 %all-reduce.3.cloned.1.call-done = (f32[96,7168]{1,0:T(8,128)}, f32[96,7168]{1,0:T(8,128)}, f32[96,7168]{1,0:T(8,128)}) async-done(((f32[96,7168]{1,0:T(8,128)}, f32[96,7168]{1,0:T(8,128)}, f32[96,7168]{1,0:T(8,128)}), (f32[96,7168]{1,0:T(8,128)}, f32[96,7168]{1,0:T(8,128)}, f32[96,7168]{1,0:T(8,128)})) %all-reduce.3.cloned.1.call-update) | async-done | bytes 8257552 | tf_op jit(solution)/shard_map/psum | solution.py:65
  259.6 10.3 %convolution_convert_fusion = bf16[7168,1024]{1,0:T(8,128)(2,1)} fusion(bf16[96,1024]{1,0:T(8,128)(2,1)S(1)} %reshape.25, f32[96,7168]{1,0:T(8,128)} %get-tuple-element.6, f32[96,7168]{1,0:T(8,128)} %get-tuple-element.4), kind=kOutput, calls=%fused_computation.3 | convolution fusion | flops 1420754944 | bytes 20381696 | tf_op jit(solution)/shard_map/dot_general | solution.py:19
  270.0 4.0 %multiply_convert_fusion.1 = (bf16[96,7168]{1,0:T(8,128)(2,1)S(1)}, bf16[96,7168]{1,0:T(8,128)(2,1)S(1)}) fusion(f32[96,7168]{1,0:T(8,128)} %get-tuple-element.5, f32[96,7168]{1,0:T(8,128)S(1)} %copy-done, f32[96,7168]{1,0:T(8,128)} %get-tuple-element.6), kind=kLoop, calls=%fused_computation.7 | loop fusion | flops 8945664 | bytes 11010048 | tf_op jit(solution)/shard_map/convert_element_type | solution.py:13
  274.0 10.3 %fusion.13 = f32[96,1024]{1,0:T(8,128)S(1)} fusion(bf16[96,7168]{1,0:T(8,128)(2,1)S(1)} %get-tuple-element.8, bf16[1024,7168]{1,0:T(8,128)(2,1)} %param.9), kind=kOutput, calls=%fused_computation.28 | convolution fusion | flops 1409286144 | bytes 16449536 | tf_op jit(solution)/shard_map/dot_general | solution.py:67
  284.3 9.9 %fusion.1 = bf16[96,1024]{1,0:T(8,128)(2,1)S(1)} fusion(f32[96,1024]{1,0:T(8,128)S(1)} %fusion.13, bf16[96,7168]{1,0:T(8,128)(2,1)S(1)} %get-tuple-element.7, bf16[1024,7168]{1,0:T(8,128)(2,1)} %param.10), kind=kOutput, calls=%fused_computation.12 | convolution fusion | flops 1409482752 | bytes 16646144 | tf_op jit(solution)/shard_map/dot_general | solution.py:70
  294.2 0.1 convert_element_type.35
  294.3 0.8 copy.42
  295.1 3.6 %all-to-all-start.4 = ((bf16[8,4,3,1024]{3,0,2,1:T(8,128)(2,1)}), bf16[8,4,3,1024]{3,0,2,1:T(8,128)(2,1)S(1)}, u32[]{:S(2)}, u32[]{:S(2)}) async-start(bf16[8,4,3,1024]{3,0,2,1:T(8,128)(2,1)} %copy.42), calls=%async_computation.4 | async-start | bytes 393216 | tf_op jit(solution)/shard_map/all_to_all | solution.py:74
  298.8 7.6 %convolution_convert_fusion.1 = bf16[1024,7168]{1,0:T(8,128)(2,1)} fusion(bf16[96,1024]{1,0:T(8,128)(2,1)S(1)} %reshape.26, bf16[96,7168]{1,0:T(8,128)(2,1)S(1)} %get-tuple-element.7), kind=kOutput, calls=%fused_computation.4 | convolution fusion | flops 1416626176 | bytes 16252928 | tf_op jit(solution)/shard_map/dot_general | solution.py:19
  306.4 0.0 all-to-all-done.4
  306.4 0.2 copy.49
  306.5 0.9 reshape.55
  307.4 5.5 %all-to-all-start.5 = ((bf16[8,1,3,4096]{3,2,1,0:T(4,128)(2,1)}), bf16[8,1,3,4096]{3,2,1,0:T(4,128)(2,1)S(1)}, u32[]{:S(2)}, u32[]{:S(2)}) async-start(bf16[8,1,3,4096]{3,2,1,0:T(4,128)(2,1)} %reshape.55), calls=%async_computation.5 | async-start | bytes 524288 | tf_op jit(solution)/shard_map/all_to_all | solution.py:73
  312.9 8.9 %convolution_convert_fusion.2 = bf16[1024,7168]{1,0:T(8,128)(2,1)} fusion(bf16[96,1024]{1,0:T(8,128)(2,1)S(1)} %reshape.26, bf16[96,7168]{1,0:T(8,128)(2,1)} %copy-done.1), kind=kOutput, calls=%fused_computation.5 | convolution fusion | flops 1416626176 | bytes 16252928 | tf_op jit(solution)/shard_map/dot_general | solution.py:19
  321.8 0.3 all-to-all-done.5
  322.2 0.2 reshape.30
  322.3 1.3 gather_fusion
  (7 shorter events, 0.1 us)
Async XLA Ops:
  21.2 16.0 %all-to-all-start.2 = ((bf16[4,2,12288]{2,1,0:T(2,128)(2,1)}), bf16[4,2,12288]{2,1,0:T(2,128)(2,1)S(1)}, u32[]{:S(2)}, u32[]{:S(2)}) async-start(bf16[4,2,12288]{2,1,0:T(2,128)(2,1)} %reshape.60), calls=%async_computation.2 | async-start | bytes 393216 | tf_op jit(solution)/shard_map/all_to_all | solution.py:43
  37.2 14.8 %all-to-all-start = ((bf16[4,2,12288]{2,1,0:T(2,128)(2,1)}), bf16[4,2,12288]{2,1,0:T(2,128)(2,1)S(1)}, u32[]{:S(2)}, u32[]{:S(2)}) async-start(bf16[4,2,12288]{2,1,0:T(2,128)(2,1)} %reshape.62), calls=%async_computation | async-start | bytes 393216 | tf_op jit(solution)/shard_map/all_to_all | solution.py:50
  52.0 17.9 %all-to-all-start.3 = ((bf16[8,4,3,1024]{3,1,2,0:T(4,128)(2,1)}), bf16[8,4,3,1024]{3,1,2,0:T(4,128)(2,1)S(1)}, u32[]{:S(2)}, u32[]{:S(2)}) async-start(bf16[8,4,3,1024]{3,1,2,0:T(4,128)(2,1)} %copy.40), calls=%async_computation.3 | async-start | bytes 393216 | tf_op jit(solution)/shard_map/all_to_all | solution.py:42
  69.9 24.8 %all-to-all-start.1 = ((bf16[8,4,3,1024]{3,1,2,0:T(4,128)(2,1)}), bf16[8,4,3,1024]{3,1,2,0:T(4,128)(2,1)S(1)}, u32[]{:S(2)}, u32[]{:S(2)}) async-start(bf16[8,4,3,1024]{3,1,2,0:T(4,128)(2,1)} %copy.36), calls=%async_computation.1 | async-start | bytes 393216 | tf_op jit(solution)/shard_map/all_to_all | solution.py:49
  75.9 183.8 %all-reduce.3.cloned.1.call-start = ((), (), s32[]{:S(2)}) async-start(), calls=%async_computation.6 | async-start | bytes 16515072 | tf_op jit(solution)/shard_map/psum | solution.py:65
  259.6 10.3 %copy-start = (f32[96,7168]{1,0:T(8,128)S(1)}, f32[96,7168]{1,0:T(8,128)}, u32[]{:S(2)}) copy-start(f32[96,7168]{1,0:T(8,128)} %get-tuple-element.4) | copy-start | bytes 8257540
  274.0 10.3 %copy-start.1 = (bf16[96,7168]{1,0:T(8,128)(2,1)}, bf16[96,7168]{1,0:T(8,128)(2,1)S(1)}, u32[]{:S(2)}) copy-start(bf16[96,7168]{1,0:T(8,128)(2,1)S(1)} %get-tuple-element.8) | copy-start | bytes 4128772
  295.1 11.2 %all-to-all-start.4 = ((bf16[8,4,3,1024]{3,0,2,1:T(8,128)(2,1)}), bf16[8,4,3,1024]{3,0,2,1:T(8,128)(2,1)S(1)}, u32[]{:S(2)}, u32[]{:S(2)}) async-start(bf16[8,4,3,1024]{3,0,2,1:T(8,128)(2,1)} %copy.42), calls=%async_computation.4 | async-start | bytes 393216 | tf_op jit(solution)/shard_map/all_to_all | solution.py:74
  307.4 14.8 %all-to-all-start.5 = ((bf16[8,1,3,4096]{3,2,1,0:T(4,128)(2,1)}), bf16[8,1,3,4096]{3,2,1,0:T(4,128)(2,1)S(1)}, u32[]{:S(2)}, u32[]{:S(2)}) async-start(bf16[8,1,3,4096]{3,2,1,0:T(4,128)(2,1)} %reshape.55), calls=%async_computation.5 | async-start | bytes 524288 | tf_op jit(solution)/shard_map/all_to_all | solution.py:73
Sparse Core Ops, SparseCore 0:
  106.5 153.1 all-reduce.2
where the time goes:
time: 332 us; the launch traced here: 330 us
  waiting for transfers between devices  154 us (46%)
  matrix products  76.6 us (23%)
  local copies, waits for them, and re-layouts  50.4 us (15%)
  starting transfers between devices  29.4 us (9%)
  between operations  14.2 us (4%)
  other arithmetic  6.24 us (2%)
    psum x1, waiting for transfers between devices, on_device(): gate, up, dhid = lax.psum((gate_part, up_part, dhid_part), 'dp')  153 us
    dot_general x3, matrix products, contract_rows(): lax.dot_general(left, right, (((0,), (0,)), ((), ())), preferred_element_...  26.9 us
    unnamed x8, local copies, waits for them, and re-layouts  21.2 us
    dot_general x1, matrix products, on_device(): lax.dot_general(rows_grad, w_down, (((1,), (1,)), ((), ())), preferred_el...  11.3 us
    dot_general x1, matrix products, on_device(): lax.dot_general(d_gate, w_gate, (((1,), (1,)), ((), ())), preferred_eleme...  10.3 us
    dot_general x1, matrix products, on_device(): lax.dot_general(d_up, w_up, (((1,), (1,)), ((), ())), preferred_element_t...  9.9 us
    another operation x4, local copies, waits for them, and re-layouts, spread(): jnp.repeat(buffer.reshape(EXPERTS, 1, capacity, width), group, axis=0)  9.43 us
    dot_general x1, matrix products, on_device(): gate_part = jnp.dot(rows_in, w_gate, preferred_element_type=jnp.float32)  9.16 us
  transfers between devices with their start and end apart: 7, of which 2 were waited for; matrix products, arithmetic and copies ran while one was open for 21% of the time, Pallas kernels for 0%

commit v1 on v0

--- a/solution.py
+++ b/solution.py
@@ -1,9 +1,21 @@
+import functools
 import jax
 import jax.numpy as jnp
 from jax import lax
 from jax.sharding import PartitionSpec as P
 
 EXPERTS = 8
+
+
+def view_values(frame_in, along_axis):
+    moved = jnp.stack(jnp.split(frame_in, jax.lax.psum(1, axis_name=along_axis), 3), axis=0)
+    heard = jnp.concatenate(
+        jax.lax.all_to_all(moved, axis_name=along_axis, split_axis=0, concat_axis=0), axis=1
+    )
+    return heard
+
+
+mix_the_units = functools.partial(view_values, along_axis="dp")
 
 
 def nonlinear(gate, up, dhid):
@@ -40,11 +52,7 @@
 
     recv_in, recv_grad = (
         lax.all_to_all(
-            lax.all_to_all(spread(inputs), "dp", split_axis=3, concat_axis=1, tiled=True),
-            "expert",
-            split_axis=0,
-            concat_axis=0,
-            tiled=True,
+            mix_the_units(spread(inputs)), "expert", split_axis=0, concat_axis=0, tiled=True
         ),
         lax.all_to_all(
             lax.all_to_all(spread(grad_out), "dp", split_axis=3, concat_axis=1, tiled=True),

time: 332 us -> 315 us (0.949)
  local copies, waits for them, and re-layouts: 50.4 us -> 30.3 us
    unnamed x8 -> x6, local copies, waits for them, and re-layouts: 21.2 us -> 10.6 us
    all_to_all x2 -> x1, local copies, waits for them, and re-layouts: 6.78 us -> 0.14 us  [on_device(): lax.all_to_all(mix_the_units(spread(inputs)), 'expert', split_axis=0, con...]
    another operation x4 -> x3, local copies, waits for them, and re-layouts: 9.43 us -> 4.84 us  [spread(): jnp.repeat(buffer.reshape(EXPERTS, 1, capacity, width), group, axis=0)]
    all_to_all x1, waiting for transfers between devices: 0.01 us -> 4.5 us  [on_device(): lax.all_to_all(spread(grad_out), 'dp', split_axis=3, concat_axis=1, tiled...]
  transfers between devices with their start and end apart: 7 -> 7, of which waited for: 2 -> 3; matrix products, arithmetic and copies ran while one was open for 21% -> 19% of each run, Pallas kernels for 0% -> 0%
where the time goes in v1:
time: 315 us; the launch traced here: 314 us
  waiting for transfers between devices  157 us (50%)
  matrix products  76.6 us (24%)
  local copies, waits for them, and re-layouts  30.3 us (10%)
  starting transfers between devices  29.3 us (9%)
  between operations  14.2 us (5%)
  other arithmetic  6.47 us (2%)
    psum x1, waiting for transfers between devices, on_device(): gate, up, dhid = lax.psum((gate_part, up_part, dhid_part), 'dp')  152 us
    dot_general x3, matrix products, contract_rows(): lax.dot_general(left, right, (((0,), (0,)), ((), ())), preferred_element_...  26.9 us
    dot_general x1, matrix products, on_device(): lax.dot_general(rows_grad, w_down, (((1,), (1,)), ((), ())), preferred_el...  11.3 us
    unnamed x6, local copies, waits for them, and re-layouts  10.6 us
    dot_general x1, matrix products, on_device(): lax.dot_general(d_gate, w_gate, (((1,), (1,)), ((), ())), preferred_eleme...  10.3 us
    dot_general x1, matrix products, on_device(): lax.dot_general(d_up, w_up, (((1,), (1,)), ((), ())), preferred_element_t...  9.9 us
    dot_general x1, matrix products, on_device(): gate_part = jnp.dot(rows_in, w_gate, preferred_element_type=jnp.float32)  9.16 us
    dot_general x1, matrix products, on_device(): up_part = jnp.dot(rows_in, w_up, preferred_element_type=jnp.float32)  9.15 us
  transfers between devices with their start and end apart: 7, of which 3 were waited for; matrix products, arithmetic and copies ran while one was open for 19% of the time, Pallas kernels for 0%

profile of v1, /device:TPU:0, one launch (start us, length us, event | category | flops | bytes accessed | tf_op | source)
XLA Modules:
  0.0 313.6 jit_solution(10159242219773479591)
XLA Ops:
  7.2 0.7 fusion.7
  7.9 0.8 select_reduce_fusion
  8.8 0.7 fusion.8
  9.4 1.2 scatter_custom_fusion.1
  10.7 0.1 reshape_broadcast_in_dim_reshape.7
  10.8 0.1 slice_bitcast_fusion.3
  10.9 0.2 pad_maximum_fusion
  11.1 0.8 copy.35
  11.9 4.2 %all-to-all-start.2 = ((bf16[4,8,1,3,1024]{4,1,3,2,0:T(8,128)(2,1)}), bf16[4,8,1,3,1024]{4,1,3,2,0:T(8,128)(2,1)S(1)}, u32[]{:S(2)}, u32[]{:S(2)}) async-start(bf16[4,8,1,3,1024]{4,1,3,2,0:T(8,128)(2,1)} %copy.35), calls=%async_computation.2 | async-start | bytes 393216 | tf_op jit(solution)/shard_map/all_to_all | solution.py:13
  16.1 1.2 scatter_custom_fusion
  17.3 0.1 reshape_broadcast_in_dim_reshape.6
  17.4 4.6 %copy.31 = bf16[8,1,3,4096]{0,2,1,3:T(4,128)(2,1)} copy(bf16[8,1,3,4096]{3,2,0,1:T(4,128)(2,1)S(1)} %reshape_broadcast_in_dim_reshape.6) | data formatting | bytes 393216 | tf_op jit(solution)/shard_map/reshape;broadcast_in_dim;reshape | solution.py:51
  22.0 5.8 %reshape.68 = bf16[4,2,12288]{2,1,0:T(2,128)(2,1)} reshape(bf16[4096,1,3,8]{3,2,1,0:T(4,128)(2,1)} %bitcast.47) | data formatting | bytes 393216
  27.9 0.0 all-to-all-done.2
  27.9 3.4 %all-to-all-start = ((bf16[4,2,12288]{2,1,0:T(2,128)(2,1)}), bf16[4,2,12288]{2,1,0:T(2,128)(2,1)S(1)}, u32[]{:S(2)}, u32[]{:S(2)}) async-start(bf16[4,2,12288]{2,1,0:T(2,128)(2,1)} %reshape.68), calls=%async_computation | async-start | bytes 393216 | tf_op jit(solution)/shard_map/all_to_all | solution.py:58
  31.3 0.8 copy.36
  32.1 4.5 %all-to-all-done = bf16[4,2,12288]{2,1,0:T(2,128)(2,1)S(1)} async-done(((bf16[4,2,12288]{2,1,0:T(2,128)(2,1)}), bf16[4,2,12288]{2,1,0:T(2,128)(2,1)S(1)}, u32[]{:S(2)}, u32[]{:S(2)}) %all-to-all-start) | async-done | bytes 196640 | tf_op jit(solution)/shard_map/all_to_all | solution.py:58
  36.6 6.4 %all-to-all-start.3 = ((bf16[8,4,3,1024]{3,1,2,0:T(4,128)(2,1)}), bf16[8,4,3,1024]{3,1,2,0:T(4,128)(2,1)S(1)}, u32[]{:S(2)}, u32[]{:S(2)}) async-start(bf16[8,4,3,1024]{3,1,2,0:T(4,128)(2,1)} %copy.36), calls=%async_computation.3 | async-start | bytes 393216 | tf_op jit(solution)/shard_map/all_to_all | solution.py:54
  43.0 4.8 %reshape.69 = bf16[4096,1,3,8]{3,2,1,0:T(4,128)(2,1)} reshape(bf16[4,2,12288]{2,1,0:T(2,128)(2,1)S(1)} %all-to-all-done) | data formatting | bytes 393216
  47.8 6.7 %copy.33 = bf16[8,4,3,1024]{3,1,2,0:T(4,128)(2,1)} copy(bf16[8,4,3,1024]{0,2,3,1:T(4,128)(2,1)} %bitcast.48) | data formatting | bytes 393216 | tf_op jit(solution)/shard_map/all_to_all | solution.py:58
  54.4 0.0 all-to-all-done.3
  54.4 6.0 %all-to-all-start.1 = ((bf16[8,4,3,1024]{3,1,2,0:T(4,128)(2,1)}), bf16[8,4,3,1024]{3,1,2,0:T(4,128)(2,1)S(1)}, u32[]{:S(2)}, u32[]{:S(2)}) async-start(bf16[8,4,3,1024]{3,1,2,0:T(4,128)(2,1)} %copy.33), calls=%async_computation.1 | async-start | bytes 393216 | tf_op jit(solution)/shard_map/all_to_all | solution.py:57
  60.4 0.2 all-reduce.3.cloned.1.call-start
  60.6 0.1 copy.37
  60.8 0.2 reshape.34
  61.0 9.2 %fusion.12 = f32[96,7168]{1,0:T(8,128)} fusion(bf16[96,1024]{1,0:T(8,128)(2,1)S(1)} %reshape.34, bf16[1024,7168]{1,0:T(8,128)(2,1)} %param.9), kind=kOutput, calls=%fused_computation.32 | convolution fusion | flops 1409286144 | bytes 17629184 | tf_op jit(solution)/shard_map/dot_general | solution.py:68
  70.1 9.2 %fusion.11 = f32[96,7168]{1,0:T(8,128)} fusion(bf16[96,1024]{1,0:T(8,128)(2,1)S(1)} %reshape.34, bf16[1024,7168]{1,0:T(8,128)(2,1)} %param.10), kind=kOutput, calls=%fused_computation.31 | convolution fusion | flops 1409286144 | bytes 17629184 | tf_op jit(solution)/shard_map/dot_general | solution.py:69
  79.3 0.0 all-to-all-done.1
  79.3 0.1 copy.34
  79.4 0.2 reshape.31
  79.6 11.3 %fusion.10 = f32[96,7168]{1,0:T(8,128)} fusion(bf16[96,1024]{1,0:T(8,128)(2,1)S(1)} %reshape.31, bf16[7168,1024]{1,0:T(8,128)(2,1)} %param.11), kind=kOutput, calls=%fused_computation.30 | convolution fusion | flops 1409286144 | bytes 17629184 | tf_op jit(solution)/shard_map/dot_general | solution.py:70
  90.9 0.0 all-reduce.3.cloned.1.call-update
  90.9 151.9 %all-reduce.3.cloned.1.call-done = (f32[96,7168]{1,0:T(8,128)}, f32[96,7168]{1,0:T(8,128)}, f32[96,7168]{1,0:T(8,128)}) async-done(((f32[96,7168]{1,0:T(8,128)}, f32[96,7168]{1,0:T(8,128)}, f32[96,7168]{1,0:T(8,128)}), (f32[96,7168]{1,0:T(8,128)}, f32[96,7168]{1,0:T(8,128)}, f32[96,7168]{1,0:T(8,128)})) %all-reduce.3.cloned.1.call-update) | async-done | bytes 8257552 | tf_op jit(solution)/shard_map/psum | solution.py:73
  242.8 10.3 %convolution_convert_fusion = bf16[7168,1024]{1,0:T(8,128)(2,1)} fusion(bf16[96,1024]{1,0:T(8,128)(2,1)S(1)} %reshape.31, f32[96,7168]{1,0:T(8,128)} %get-tuple-element.6, f32[96,7168]{1,0:T(8,128)} %get-tuple-element.4), kind=kOutput, calls=%fused_computation.3 | convolution fusion | flops 1420754944 | bytes 20381696 | tf_op jit(solution)/shard_map/dot_general | solution.py:31
  253.1 4.0 %multiply_convert_fusion.1 = (bf16[96,7168]{1,0:T(8,128)(2,1)S(1)}, bf16[96,7168]{1,0:T(8,128)(2,1)S(1)}) fusion(f32[96,7168]{1,0:T(8,128)} %get-tuple-element.5, f32[96,7168]{1,0:T(8,128)S(1)} %copy-done, f32[96,7168]{1,0:T(8,128)} %get-tuple-element.6), kind=kLoop, calls=%fused_computation.7 | loop fusion | flops 8945664 | bytes 11010048 | tf_op jit(solution)/shard_map/convert_element_type | solution.py:25
  257.1 10.3 %fusion.13 = f32[96,1024]{1,0:T(8,128)S(1)} fusion(bf16[96,7168]{1,0:T(8,128)(2,1)S(1)} %get-tuple-element.8, bf16[1024,7168]{1,0:T(8,128)(2,1)} %param.9), kind=kOutput, calls=%fused_computation.33 | convolution fusion | flops 1409286144 | bytes 16449536 | tf_op jit(solution)/shard_map/dot_general | solution.py:75
  267.4 9.9 %fusion.1 = bf16[96,1024]{1,0:T(8,128)(2,1)S(1)} fusion(f32[96,1024]{1,0:T(8,128)S(1)} %fusion.13, bf16[96,7168]{1,0:T(8,128)(2,1)S(1)} %get-tuple-element.7, bf16[1024,7168]{1,0:T(8,128)(2,1)} %param.10), kind=kOutput, calls=%fused_computation.12 | convolution fusion | flops 1409482752 | bytes 16646144 | tf_op jit(solution)/shard_map/dot_general | solution.py:78
  277.3 0.1 convert_element_type.35
  277.4 0.8 copy.38
  278.3 3.6 %all-to-all-start.4 = ((bf16[8,4,3,1024]{3,0,2,1:T(8,128)(2,1)}), bf16[8,4,3,1024]{3,0,2,1:T(8,128)(2,1)S(1)}, u32[]{:S(2)}, u32[]{:S(2)}) async-start(bf16[8,4,3,1024]{3,0,2,1:T(8,128)(2,1)} %copy.38), calls=%async_computation.4 | async-start | bytes 393216 | tf_op jit(solution)/shard_map/all_to_all | solution.py:82
  281.9 7.6 %convolution_convert_fusion.1 = bf16[1024,7168]{1,0:T(8,128)(2,1)} fusion(bf16[96,1024]{1,0:T(8,128)(2,1)S(1)} %reshape.34, bf16[96,7168]{1,0:T(8,128)(2,1)S(1)} %get-tuple-element.7), kind=kOutput, calls=%fused_computation.4 | convolution fusion | flops 1416626176 | bytes 16252928 | tf_op jit(solution)/shard_map/dot_general | solution.py:31
  289.5 0.2 copy.43
  289.6 0.9 reshape.63
  290.5 5.5 %all-to-all-start.5 = ((bf16[8,1,3,4096]{3,2,1,0:T(4,128)(2,1)}), bf16[8,1,3,4096]{3,2,1,0:T(4,128)(2,1)S(1)}, u32[]{:S(2)}, u32[]{:S(2)}) async-start(bf16[8,1,3,4096]{3,2,1,0:T(4,128)(2,1)} %reshape.63), calls=%async_computation.5 | async-start | bytes 524288 | tf_op jit(solution)/shard_map/all_to_all | solution.py:81
  296.0 8.9 %convolution_convert_fusion.2 = bf16[1024,7168]{1,0:T(8,128)(2,1)} fusion(bf16[96,1024]{1,0:T(8,128)(2,1)S(1)} %reshape.34, bf16[96,7168]{1,0:T(8,128)(2,1)} %copy-done.1), kind=kOutput, calls=%fused_computation.5 | convolution fusion | flops 1416626176 | bytes 16252928 | tf_op jit(solution)/shard_map/dot_general | solution.py:31
  305.0 0.3 all-to-all-done.5
  305.3 0.2 reshape.38
  305.5 1.3 gather_fusion
  (7 shorter events, 0.1 us)
Async XLA Ops:
  11.9 16.0 %all-to-all-start.2 = ((bf16[4,8,1,3,1024]{4,1,3,2,0:T(8,128)(2,1)}), bf16[4,8,1,3,1024]{4,1,3,2,0:T(8,128)(2,1)S(1)}, u32[]{:S(2)}, u32[]{:S(2)}) async-start(bf16[4,8,1,3,1024]{4,1,3,2,0:T(8,128)(2,1)} %copy.35), calls=%async_computation.2 | async-start | bytes 393216 | tf_op jit(solution)/shard_map/all_to_all | solution.py:13
  27.9 8.7 %all-to-all-start = ((bf16[4,2,12288]{2,1,0:T(2,128)(2,1)}), bf16[4,2,12288]{2,1,0:T(2,128)(2,1)S(1)}, u32[]{:S(2)}, u32[]{:S(2)}) async-start(bf16[4,2,12288]{2,1,0:T(2,128)(2,1)} %reshape.68), calls=%async_computation | async-start | bytes 393216 | tf_op jit(solution)/shard_map/all_to_all | solution.py:58
  36.6 17.8 %all-to-all-start.3 = ((bf16[8,4,3,1024]{3,1,2,0:T(4,128)(2,1)}), bf16[8,4,3,1024]{3,1,2,0:T(4,128)(2,1)S(1)}, u32[]{:S(2)}, u32[]{:S(2)}) async-start(bf16[8,4,3,1024]{3,1,2,0:T(4,128)(2,1)} %copy.36), calls=%async_computation.3 | async-start | bytes 393216 | tf_op jit(solution)/shard_map/all_to_all | solution.py:54
  54.4 24.8 %all-to-all-start.1 = ((bf16[8,4,3,1024]{3,1,2,0:T(4,128)(2,1)}), bf16[8,4,3,1024]{3,1,2,0:T(4,128)(2,1)S(1)}, u32[]{:S(2)}, u32[]{:S(2)}) async-start(bf16[8,4,3,1024]{3,1,2,0:T(4,128)(2,1)} %copy.33), calls=%async_computation.1 | async-start | bytes 393216 | tf_op jit(solution)/shard_map/all_to_all | solution.py:57
  60.4 182.4 %all-reduce.3.cloned.1.call-start = ((), (), s32[]{:S(2)}) async-start(), calls=%async_computation.6 | async-start | bytes 16515072 | tf_op jit(solution)/shard_map/psum | solution.py:73
  242.8 10.3 %copy-start = (f32[96,7168]{1,0:T(8,128)S(1)}, f32[96,7168]{1,0:T(8,128)}, u32[]{:S(2)}) copy-start(f32[96,7168]{1,0:T(8,128)} %get-tuple-element.4) | copy-start | bytes 8257540
  257.1 10.3 %copy-start.1 = (bf16[96,7168]{1,0:T(8,128)(2,1)}, bf16[96,7168]{1,0:T(8,128)(2,1)S(1)}, u32[]{:S(2)}) copy-start(bf16[96,7168]{1,0:T(8,128)(2,1)S(1)} %get-tuple-element.8) | copy-start | bytes 4128772
  278.3 11.2 %all-to-all-start.4 = ((bf16[8,4,3,1024]{3,0,2,1:T(8,128)(2,1)}), bf16[8,4,3,1024]{3,0,2,1:T(8,128)(2,1)S(1)}, u32[]{:S(2)}, u32[]{:S(2)}) async-start(bf16[8,4,3,1024]{3,0,2,1:T(8,128)(2,1)} %copy.38), calls=%async_computation.4 | async-start | bytes 393216 | tf_op jit(solution)/shard_map/all_to_all | solution.py:82
  290.5 14.8 %all-to-all-start.5 = ((bf16[8,1,3,4096]{3,2,1,0:T(4,128)(2,1)}), bf16[8,1,3,4096]{3,2,1,0:T(4,128)(2,1)S(1)}, u32[]{:S(2)}, u32[]{:S(2)}) async-start(bf16[8,1,3,4096]{3,2,1,0:T(4,128)(2,1)} %reshape.63), calls=%async_computation.5 | async-start | bytes 524288 | tf_op jit(solution)/shard_map/all_to_all | solution.py:81
Sparse Core Ops, SparseCore 0:
  91.0 151.7 all-reduce.2
